TPU v7x, 256 devices: a whole 4x4x8 slice. The times are simulated.
256 devices in a mesh: seq: 16 (over x, y), grp: 16 (over z, core).
Axes of the slice: x: 4, y: 4, z: 8, core: 2. Of those that a mesh axis runs over, the one named last changes fastest.
Arguments:
- query_rows: bfloat16 [16, 2048, 4096], P('grp', 'seq'), may hold values from -6 to 6
- key_rows: bfloat16 [16, 2048, 1024], P('grp', 'seq'), may hold values from -6 to 6
- value_rows: bfloat16 [16, 2048, 1024], P('grp', 'seq'), may hold values from -27 to 27
- doc_of_block: int32 [16, 16], P('grp'), may hold values from 0 to 3, never falling along the last dimension, each value on 1 to 8 neighbouring positions
- expert_ids: int32 [16, 2048, 2], P('grp', 'seq'), may hold values from 0 to 7, as said below
- gate_weights: float32 [16, 2048, 2], P('grp', 'seq'), may hold values from 0.1 to 0.9
- norm_gain: float32 [4096], replicated, may hold values from 0.1 to 1.9
- w_in: bfloat16 [2, 7168, 4096], P(None, ('seq', 'grp')), may hold values from -0.09375 to 0.09375
- w_down: bfloat16 [7168, 4096], P(('seq', 'grp')), may hold values from -0.0625 to 0.0625
Outputs:
- layer_out: bfloat16 [16, 2048, 4096], P('grp', 'seq')
Inputs may be any that keep to these rules, and one draw needn't show every extreme that they name: `expert_ids`: each token names 2 different experts; in each aligned block of 128 tokens along a sequence (the tokens of one device) at most 40 tokens name expert 0, and in every draw some block has exactly 40 such tokens.
All inputs are finite; a program needn't handle non-finite values.
Results may differ from a plain program's by a relative error of at most 0.014.
Values may be sent and summed in bfloat16 or wider, within the bound.
No kernel may reach another device: no remote copies, remote signals or barrier semaphores. Data moves between devices by JAX's collectives and lax.ppermute only.
A program may use at most 128 MiB of HBM per device.

v0:
```python
import math
import jax
import jax.numpy as jnp
from jax import lax
from jax.sharding import PartitionSpec as P

QH = 32
KVH = 8
HD = 128
BLK = 128
CAP = 40
EPS = 1e-05
NEG = -1e30


def project_in(gathered, piece):
    return jnp.einsum("rd,khd->krh", gathered, piece, preferred_element_type=jnp.float32)


def activate(gate_up):
    return (jax.nn.silu(gate_up[0]) * gate_up[1]).astype(jnp.bfloat16)


def add_down(hidden, piece):
    return jnp.dot(hidden, piece, preferred_element_type=jnp.float32)


def attend(query_all, key_all, value_all, token_doc, per_dev, kv_local):
    seq_length = query_all.shape[1]
    tile_rows = min(512, seq_length)
    tile_count = seq_length // tile_rows
    per_kv = per_dev // kv_local
    inv_root = 1.0 / math.sqrt(HD)
    query_split = query_all[0].reshape(seq_length, kv_local, per_kv, HD)
    key_split = key_all[0].reshape(seq_length, kv_local, HD)
    value_split = value_all[0].reshape(seq_length, kv_local, HD)
    outputs = []
    for q_index in range(tile_count):
        query_tile = query_split[q_index * tile_rows : (q_index + 1) * tile_rows]
        doc_query = token_doc[q_index * tile_rows : (q_index + 1) * tile_rows]
        allowed_row = doc_query[:, None] == token_doc[None, :]
        scores = (
            jnp.einsum("qkgd,tkd->kgqt", query_tile, key_split, preferred_element_type=jnp.float32)
            * inv_root
        )
        scores = jnp.where(allowed_row, scores, NEG)
        highest = jnp.max(scores, axis=3, keepdims=True)
        weights = jnp.exp(scores - highest)
        denom = jnp.sum(weights, axis=3, keepdims=True)
        mixed = jnp.einsum(
            "kgqt,tkd->qkgd",
            weights.astype(jnp.bfloat16),
            value_split,
            preferred_element_type=jnp.float32,
        )
        mixed = mixed / jnp.transpose(denom, (2, 0, 1, 3))
        outputs.append(mixed.reshape(tile_rows, per_dev * HD).astype(jnp.bfloat16))
    return jnp.concatenate(outputs, axis=0)[None]


def shards(
    query_rows,
    key_rows,
    value_rows,
    doc_of_block,
    expert_ids,
    gate_weights,
    norm_gain,
    w_in,
    w_down,
):
    seq_count = lax.axis_size("seq")
    tok_count = query_rows.shape[1]
    per_dev = QH // seq_count
    repeat_count = max(1, 4 // per_dev)
    kv_local = KVH * repeat_count // seq_count
    key_send = jnp.repeat(key_rows.reshape(1, tok_count, KVH, HD), repeat_count, axis=2).reshape(
        1, tok_count, KVH * repeat_count * HD
    )
    value_send = jnp.repeat(
        value_rows.reshape(1, tok_count, KVH, HD), repeat_count, axis=2
    ).reshape(1, tok_count, KVH * repeat_count * HD)
    query_all, key_all, value_all = (
        lax.all_to_all(query_rows, "seq", split_axis=2, concat_axis=1, tiled=True),
        lax.all_to_all(key_send, "seq", split_axis=2, concat_axis=1, tiled=True),
        lax.all_to_all(value_send, "seq", split_axis=2, concat_axis=1, tiled=True),
    )
    token_doc = jnp.repeat(doc_of_block[0], BLK)
    attended = attend(query_all, key_all, value_all, token_doc, per_dev, kv_local)
    attn_tokens = lax.all_to_all(attended, "seq", split_axis=1, concat_axis=2, tiled=True)
    attn_float = attn_tokens[0].astype(jnp.float32)
    spread = jnp.mean(attn_float * attn_float, axis=-1, keepdims=True)
    normed = (attn_float * lax.rsqrt(spread + EPS) * norm_gain).astype(jnp.bfloat16)
    chosen = expert_ids[0] == 0
    routed = jnp.any(chosen, axis=-1)
    gate_share = jnp.sum(jnp.where(chosen, gate_weights[0], 0.0), axis=-1)
    slot_index = jnp.cumsum(routed.astype(jnp.int32)) - 1
    onehot = (slot_index[None, :] == jnp.arange(CAP, dtype=jnp.int32)[:, None]) & routed[None, :]
    dispatched = jnp.dot(
        onehot.astype(jnp.bfloat16), normed, preferred_element_type=jnp.float32
    ).astype(jnp.bfloat16)
    gathered = lax.all_gather(dispatched, "grp", axis=0, tiled=True)
    gate_up = project_in(gathered, lax.all_gather(w_in, "seq", axis=1, tiled=True))
    hidden = activate(gate_up)
    terms = add_down(hidden, lax.all_gather(w_down, "seq", axis=0, tiled=True))
    returned = lax.psum_scatter(
        terms.astype(jnp.bfloat16), "grp", scatter_dimension=0, tiled=True
    ).astype(jnp.float32)
    picked_rows = jnp.take(returned, jnp.clip(slot_index, 0, CAP - 1), axis=0)
    expert_out = jnp.where(routed[:, None], picked_rows, 0.0)
    layer_out = attn_float + gate_share[:, None] * expert_out
    return layer_out.astype(jnp.bfloat16)[None]


def solution(mesh):
    return jax.shard_map(
        shards,
        mesh=mesh,
        in_specs=(
            P("grp", "seq", None),
            P("grp", "seq", None),
            P("grp", "seq", None),
            P("grp", None),
            P("grp", "seq", None),
            P("grp", "seq", None),
            P(),
            P(None, ("seq", "grp"), None),
            P(("seq", "grp"), None),
        ),
        out_specs=P("grp", "seq", None),
        check_vma=False,
    )
```

profile of v0, /device:TPU:2, one launch (start us, length us, event | category | flops | bytes accessed | tf_op | source)
XLA Modules:
  0.0 441.8 jit_solution(3743156761703894871)
XLA Ops:
  6.5 1.2 copy.112
  7.9 8.1 %copy.145 = bf16[1,128,2048]{1,0,2:T(2,128)(2,1)S(1)} copy(bf16[1,128,2048]{1,2,0:T(8,128)(2,1)S(1)} %bitcast.306) | data formatting | bytes 1048576 | tf_op jit(solution)/shard_map/broadcast_in_dim | solution.py:77
  16.5 11.5 %reduce.20 = bf16[2048,128]{1,0:T(8,128)(2,1)S(1)} reduce(bf16[2048,1,128]{2,1,0:T(2,128)(2,1)S(1)} %bitcast.304, bf16[]{:T(256)} %broadcast.226), dimensions={1}, to_apply=%bitcast.292.reduce_sub_computation | reduce | bytes 1048578
  29.0 7.5 %all-to-all-start = ((bf16[16,2,8192]{2,1,0:T(2,128)(2,1)}), bf16[16,2,8192]{2,1,0:T(2,128)(2,1)S(1)}, u32[]{:S(2)}, u32[]{:S(2)}) async-start(bf16[16,2,8192]{2,1,0:T(2,128)(2,1)} %reshape.333), calls=%async_computation | async-start | bytes 1048576 | tf_op jit(solution)/shard_map/all_to_all | solution.py:85
  36.5 10.8 %all-gather.9.cloned.1.call-start = ((), (), s32[]{:S(2)}) async-start(), calls=%async_computation.8 | async-start | bytes 4456448 | tf_op jit(solution)/shard_map/all_gather | solution.py:105
  47.3 1.1 copy.113
  48.5 8.1 %copy.144 = bf16[1,128,2048]{1,0,2:T(2,128)(2,1)S(1)} copy(bf16[1,128,2048]{1,2,0:T(8,128)(2,1)S(1)} %bitcast.307) | data formatting | bytes 1048576 | tf_op jit(solution)/shard_map/broadcast_in_dim | solution.py:80
  56.6 11.5 %reduce.19 = bf16[2048,128]{1,0:T(8,128)(2,1)S(1)} reduce(bf16[2048,1,128]{2,1,0:T(2,128)(2,1)S(1)} %bitcast.305, bf16[]{:T(256)} %broadcast.226), dimensions={1}, to_apply=%bitcast.291.reduce_sub_computation | reduce | bytes 1048578
  69.1 7.2 %all-to-all-start.2 = ((bf16[16,2,8192]{2,1,0:T(2,128)(2,1)}), bf16[16,2,8192]{2,1,0:T(2,128)(2,1)}, u32[]{:S(2)}, u32[]{:S(2)}) async-start(bf16[16,2,8192]{2,1,0:T(2,128)(2,1)} %reshape.331), calls=%async_computation.2 | async-start | bytes 1048576 | tf_op jit(solution)/shard_map/all_to_all | solution.py:86
  76.4 2.8 copy.84
  79.2 22.4 %reduce.21 = bf16[4096,128]{1,0:T(8,128)(2,1)S(1)} reduce(bf16[4096,1,128]{2,1,0:T(2,128)(2,1)S(1)} %bitcast.299, bf16[]{:T(256)} %broadcast.226), dimensions={1}, to_apply=%bitcast.272.reduce_sub_computation | reduce | bytes 2097154
  101.6 1.1 reshape.335
  102.9 7.7 %all-to-all-start.1 = ((bf16[16,2,16384]{2,1,0:T(2,128)(2,1)}), bf16[16,2,16384]{2,1,0:T(2,128)(2,1)S(1)}, u32[]{:S(2)}, u32[]{:S(2)}) async-start(bf16[16,2,16384]{2,1,0:T(2,128)(2,1)} %reshape.335), calls=%async_computation.1 | async-start | bytes 2097152 | tf_op jit(solution)/shard_map/all_to_all | solution.py:84
  110.7 3.8 broadcast_compare_fusion.3
  114.5 2.2 reshape.334
  117.8 2.2 reshape.332
  121.5 3.1 all-to-all-done.1
  126.1 3.3 fusion.10
  129.4 2.0 fusion
  131.5 2.6 fusion.59
  134.4 2.9 fusion.11
  137.4 2.2 fusion.2
  139.6 2.6 fusion.65
  142.6 2.9 fusion.12
  145.5 2.0 fusion.4
  147.6 3.3 fusion.71
  152.2 2.2 fusion.13
  154.4 2.2 fusion.6
  156.7 2.6 fusion.77
  159.5 11.7 %copy.143 = bf16[1,2048,256]{2,0,1:T(2,128)(2,1)S(1)} copy(bf16[1,2048,256]{2,1,0:T(8,128)(2,1)S(1)} %maximum_bitcast_fusion) | data formatting | bytes 2097152 | tf_op jit(solution)/shard_map/broadcast_in_dim | solution.py:58
  171.3 10.6 %reduce.22 = bf16[2048,256]{1,0:T(8,128)(2,1)S(1)} reduce(bf16[2048,1,256]{2,1,0:T(2,128)(2,1)S(1)} %bitcast.297, bf16[]{:T(256)} %broadcast.226), dimensions={1}, to_apply=%bitcast.290.reduce_sub_computation | reduce | bytes 2097154
  181.9 1.1 reshape.337
  183.0 5.6 %all-to-all-start.3 = ((bf16[16,2,16384]{2,1,0:T(2,128)(2,1)}), bf16[16,2,16384]{2,1,0:T(2,128)(2,1)S(1)}, u32[]{:S(2)}, u32[]{:S(2)}) async-start(bf16[16,2,16384]{2,1,0:T(2,128)(2,1)} %reshape.337), calls=%async_computation.3 | async-start | bytes 2097152 | tf_op jit(solution)/shard_map/all_to_all | solution.py:90
  189.1 13.6 %all-to-all-done.3 = bf16[16,2,16384]{2,1,0:T(2,128)(2,1)S(1)} async-done(((bf16[16,2,16384]{2,1,0:T(2,128)(2,1)}), bf16[16,2,16384]{2,1,0:T(2,128)(2,1)S(1)}, u32[]{:S(2)}, u32[]{:S(2)}) %all-to-all-start.3) | async-done | bytes 1048608 | tf_op jit(solution)/shard_map/all_to_all | solution.py:90
  203.7 1.2 copy.105
  205.0 1.6 copy.117
  206.6 15.4 %multiply_reduce_fusion = f32[2048]{0:T(1024)S(1)} fusion(bf16[2048,1,256]{2,1,0:T(2,128)(2,1)S(1)} %reshape.338), kind=kLoop, calls=%fused_computation.44 | loop fusion | flops 1570816 | bytes 1056768 | tf_op jit(solution)/shard_map/reduce_sum | solution.py:92
  222.1 1.1 convolution_convert_fusion.1
  224.0 5.1 %reshape.324 = bf16[448,4096]{1,0:T(8,128)(2,1)} reshape(bf16[16,28,4096]{2,1,0:T(8,128)(2,1)} %all-gather.9.cloned.1.call-done) | data formatting | bytes 7340032
  229.1 38.4 %all-gather.5.cloned.1.call-done = bf16[640,4096]{1,0:T(8,128)(2,1)} async-done(((bf16[40,4096]{1,0:T(8,128)(2,1)}), bf16[640,4096]{1,0:T(8,128)(2,1)}) %all-gather.5.cloned.1.call-update) | async-done | bytes 5242896 | tf_op jit(solution)/shard_map/all_gather | solution.py:102
  267.5 72.1 %all-gather.7.cloned.1.call-done = bf16[2,448,4096]{2,0,1:T(2,128)(2,1)} async-done(((bf16[2,28,4096]{2,0,1:T(2,128)(2,1)}), bf16[2,448,4096]{2,0,1:T(2,128)(2,1)}) %all-gather.7.cloned.1.call-update) | async-done | bytes 7340048 | tf_op jit(solution)/shard_map/all_gather | solution.py:103
  339.6 18.5 %fusion.35 = f32[2,640,448]{1,2,0:T(8,128)S(1)} fusion(bf16[2,448,4096]{2,0,1:T(2,128)(2,1)} %all-gather.7.cloned.1.call-done, bf16[640,4096]{1,0:T(8,128)(2,1)} %all-gather.5.cloned.1.call-done), kind=kOutput, calls=%fused_computation.49 | convolution fusion | flops 4697620480 | bytes 14876672 | tf_op jit(solution)/shard_map/rd,khd->krh/dot_general | solution.py:17
  358.2 4.8 %convolution_convert_fusion = bf16[640,4096]{1,0:T(8,128)(2,1)} fusion(bf16[448,4096]{1,0:T(8,128)(2,1)S(1)} %copy-done.4, f32[2,640,448]{1,2,0:T(8,128)S(1)} %fusion.35), kind=kOutput, calls=%fused_computation.23 | convolution fusion | flops 2353152000 | bytes 11206656 | tf_op jit(solution)/shard_map/dot_general | solution.py:25
  363.0 2.6 copy.142
  365.6 1.7 reshape.310
  367.4 60.8 %reduce-scatter.2.cloned.1.call-done = bf16[40,4096]{1,0:T(8,128)(2,1)} async-done(((bf16[640,4096]{1,0:T(8,128)(2,1)}), bf16[40,4096]{1,0:T(8,128)(2,1)}) %reduce-scatter.2.cloned.1.call-update) | async-done | bytes 327696 | tf_op jit(solution)/shard_map/reduce_scatter | solution.py:106
  429.2 2.6 gather_fusion
  431.7 3.1 fusion.34
  (84 shorter events, 12.5 us)
Async XLA Ops:
  6.5 69.8 %copy-start.13 = (s32[1,16]{1,0:T(1,128)S(1)}, s32[1,16]{1,0:T(1,128)}, u32[]{:S(2)}) copy-start(s32[1,16]{1,0:T(1,128)} %param.12) | copy-start | bytes 196
  6.5 69.9 %copy-start.6 = (bf16[1,128,4096]{2,1,0:T(8,128)(2,1)S(1)}, bf16[1,128,4096]{2,1,0:T(8,128)(2,1)}, u32[]{:S(2)}) copy-start(bf16[1,128,4096]{2,1,0:T(8,128)(2,1)} %param.9) | copy-start | bytes 3145732
  29.0 40.1 %all-to-all-start = ((bf16[16,2,8192]{2,1,0:T(2,128)(2,1)}), bf16[16,2,8192]{2,1,0:T(2,128)(2,1)S(1)}, u32[]{:S(2)}, u32[]{:S(2)}) async-start(bf16[16,2,8192]{2,1,0:T(2,128)(2,1)} %reshape.333), calls=%async_computation | async-start | bytes 1048576 | tf_op jit(solution)/shard_map/all_to_all | solution.py:85
  36.5 187.5 %all-gather.9.cloned.1.call-start = ((), (), s32[]{:S(2)}) async-start(), calls=%async_computation.8 | async-start | bytes 4456448 | tf_op jit(solution)/shard_map/all_gather | solution.py:105
  69.1 7.2 %copy-start.5 = (bf16[16,2,8192]{2,1,0:T(2,128)(2,1)}, bf16[16,2,8192]{2,1,0:T(2,128)(2,1)S(1)}, u32[]{:S(2)}) copy-start(bf16[16,2,8192]{2,1,0:T(2,128)(2,1)S(1)} %all-to-all-done) | copy-start | bytes 1572868
  69.1 33.8 %all-to-all-start.2 = ((bf16[16,2,8192]{2,1,0:T(2,128)(2,1)}), bf16[16,2,8192]{2,1,0:T(2,128)(2,1)}, u32[]{:S(2)}, u32[]{:S(2)}) async-start(bf16[16,2,8192]{2,1,0:T(2,128)(2,1)} %reshape.331), calls=%async_computation.2 | async-start | bytes 1048576 | tf_op jit(solution)/shard_map/all_to_all | solution.py:86
  102.9 21.7 %all-to-all-start.1 = ((bf16[16,2,16384]{2,1,0:T(2,128)(2,1)}), bf16[16,2,16384]{2,1,0:T(2,128)(2,1)S(1)}, u32[]{:S(2)}, u32[]{:S(2)}) async-start(bf16[16,2,16384]{2,1,0:T(2,128)(2,1)} %reshape.335), calls=%async_computation.1 | async-start | bytes 2097152 | tf_op jit(solution)/shard_map/all_to_all | solution.py:84
  125.8 3.6 copy-start.3
  126.1 5.3 %copy-start.8 = (bf16[2048,128,1]{0,1,2:T(8,128)(2,1)S(1)}, bf16[2048,128,1]{0,1,2:T(8,128)(2,1)}, u32[]{:S(2)}) copy-start(bf16[2048,128,1]{0,1,2:T(8,128)(2,1)} %reshape.326) | copy-start | bytes 1572868
  131.4 3.0 copy-start.2
  134.4 5.1 %copy-start.9 = (bf16[2048,128,1]{0,1,2:T(8,128)(2,1)S(1)}, bf16[2048,128,1]{0,1,2:T(8,128)(2,1)}, u32[]{:S(2)}) copy-start(bf16[2048,128,1]{0,1,2:T(8,128)(2,1)} %reshape.326) | copy-start | bytes 1572868
  139.6 3.0 copy-start.1
  142.6 5.0 %copy-start.10 = (bf16[2048,128,1]{0,1,2:T(8,128)(2,1)S(1)}, bf16[2048,128,1]{0,1,2:T(8,128)(2,1)}, u32[]{:S(2)}) copy-start(bf16[2048,128,1]{0,1,2:T(8,128)(2,1)} %reshape.326) | copy-start | bytes 1572868
  147.5 4.6 %copy-start = (pred[512,2048]{0,1:T(8,128)(4,1)S(1)}, pred[512,2048]{0,1:T(8,128)(4,1)}, u32[]{:S(2)}) copy-start(pred[512,2048]{0,1:T(8,128)(4,1)} %get-tuple-element.14) | copy-start | bytes 3145732
  147.6 4.6 %copy-start.7 = (bf16[1,16,128,128]{3,2,1,0:T(8,128)(2,1)S(1)}, bf16[1,16,128,128]{3,2,1,0:T(8,128)(2,1)}, u32[]{:S(2)}) copy-start(bf16[1,16,128,128]{3,2,1,0:T(8,128)(2,1)} %copy.83) | copy-start | bytes 1572868
  152.2 4.5 %copy-start.11 = (bf16[2048,128,1]{0,1,2:T(8,128)(2,1)S(1)}, bf16[2048,128,1]{0,1,2:T(8,128)(2,1)}, u32[]{:S(2)}) copy-start(bf16[2048,128,1]{0,1,2:T(8,128)(2,1)} %reshape.326) | copy-start | bytes 1572868
  159.3 29.3 %copy-start.14 = (s32[1,128,2]{1,2,0:T(2,128)S(1)}, s32[1,128,2]{1,2,0:T(2,128)}, u32[]{:S(2)}) copy-start(s32[1,128,2]{1,2,0:T(2,128)} %param.13) | copy-start | bytes 3076
  183.0 39.1 %copy-start.12 = (f32[4096]{0:T(1024)S(1)}, f32[4096]{0:T(1024)}, u32[]{:S(2)}) copy-start(f32[4096]{0:T(1024)} %param.15) | copy-start | bytes 49156
  183.0 19.7 %all-to-all-start.3 = ((bf16[16,2,16384]{2,1,0:T(2,128)(2,1)}), bf16[16,2,16384]{2,1,0:T(2,128)(2,1)S(1)}, u32[]{:S(2)}, u32[]{:S(2)}) async-start(bf16[16,2,16384]{2,1,0:T(2,128)(2,1)} %reshape.337), calls=%async_computation.3 | async-start | bytes 2097152 | tf_op jit(solution)/shard_map/all_to_all | solution.py:90
  188.6 78.9 %all-gather.5.cloned.1.call-start = ((), (), s32[]{:S(2)}) async-start(), calls=%async_computation.5 | async-start | bytes 5570560 | tf_op jit(solution)/shard_map/all_gather | solution.py:102
  223.2 116.4 %all-gather.7.cloned.1.call-start = ((), (), s32[]{:S(2)}) async-start(), calls=%async_computation.6 | async-start | bytes 7798784 | tf_op jit(solution)/shard_map/all_gather | solution.py:103
  223.9 204.2 %reduce-scatter.2.cloned.1.call-start = ((), (), s32[]{:S(2)}) async-start(), calls=%async_computation.7 | async-start | bytes 5570560 | tf_op jit(solution)/shard_map/reduce_scatter | solution.py:106
  339.6 18.6 %copy-start.4 = (bf16[448,4096]{1,0:T(8,128)(2,1)S(1)}, bf16[448,4096]{1,0:T(8,128)(2,1)}, u32[]{:S(2)}) copy-start(bf16[448,4096]{1,0:T(8,128)(2,1)} %reshape.324) | copy-start | bytes 11010052
  358.2 4.8 %copy-start.15 = (f32[1,128,2]{1,2,0:T(2,128)S(1)}, f32[1,128,2]{1,2,0:T(2,128)}, u32[]{:S(2)}) copy-start(f32[1,128,2]{1,2,0:T(2,128)} %param.14) | copy-start | bytes 3076
Sparse Core Ops, SparseCore 0:
  47.4 59.1 all-gather.8
  223.3 44.1 all-gather.4
  270.0 69.6 all-gather.6
  363.1 64.9 reduce-scatter.1
where the time goes:
time: 450 us; the launch traced here: 442 us
  waiting for transfers between devices  189 us (42%)
  other arithmetic  88.2 us (20%)
  local copies, waits for them, and re-layouts  64.8 us (14%)
  matrix products  46.9 us (10%)
  starting transfers between devices  38.9 us (9%)
  between operations  14.1 us (3%)
    all_gather x1, waiting for transfers between devices, shards(): lax.all_gather(w_in, 'seq', axis=1, tiled=True)  72.1 us
    reduce_scatter x1, waiting for transfers between devices, shards(): lax.psum_scatter(terms.astype(jnp.bfloat16), 'grp', scatter_dimension=0,...  60.8 us
    unnamed x4, other arithmetic  56 us
    all_gather x1, waiting for transfers between devices, shards(): gathered = lax.all_gather(dispatched, 'grp', axis=0, tiled=True)  38.4 us
    unnamed x47, local copies, waits for them, and re-layouts  21 us
    dot_general x1, matrix products, project_in(): jnp.einsum('rd,khd->krh', gathered, piece, preferred_element_type=jnp.flo...  18.5 us
    reduce_sum x2, other arithmetic, shards(): spread = jnp.mean(attn_float * attn_float, axis=-1, keepdims=True)  15.4 us
    all_to_all x1, waiting for transfers between devices, shards(): lax.all_to_all(attended, 'seq', split_axis=1, concat_axis=2, tiled=True)  13.6 us
  transfers between devices with their start and end apart: 8, of which 5 were waited for; matrix products, arithmetic and copies ran while one was open for 33% of the time, Pallas kernels for 0%

commit v1 on v0

--- a/solution.py
+++ b/solution.py
@@ -11,6 +11,13 @@
 CAP = 40
 EPS = 1e-05
 NEG = -1e30
+
+
+def swap_blocks(shard, mesh_axis, split, join):
+    size = lax.axis_size(mesh_axis)
+    blocks = jnp.stack(jnp.split(shard, size, axis=split), axis=0)
+    blocks = lax.all_to_all(blocks, mesh_axis, split_axis=0, concat_axis=0)
+    return jnp.concatenate(blocks, axis=join)
 
 
 def project_in(gathered, piece):
@@ -87,7 +94,7 @@
     )
     token_doc = jnp.repeat(doc_of_block[0], BLK)
     attended = attend(query_all, key_all, value_all, token_doc, per_dev, kv_local)
-    attn_tokens = lax.all_to_all(attended, "seq", split_axis=1, concat_axis=2, tiled=True)
+    attn_tokens = swap_blocks(attended, "seq", 1, 2)
     attn_float = attn_tokens[0].astype(jnp.float32)
     spread = jnp.mean(attn_float * attn_float, axis=-1, keepdims=True)
     normed = (attn_float * lax.rsqrt(spread + EPS) * norm_gain).astype(jnp.bfloat16)

time: 450 us -> 405 us (0.900)
  other arithmetic: 88.2 us -> 65 us
  starting transfers between devices: 38.9 us -> 28.2 us
  local copies, waits for them, and re-layouts: 64.8 us -> 54.6 us
    reduce_sum x2 -> x1, other arithmetic: 15.4 us -> 0.56 us  [shards(): spread = jnp.mean(attn_float * attn_float, axis=-1, keepdims=True)]
    broadcast_in_dim x1 -> x0, local copies, waits for them, and re-layouts: 11.7 us -> none  [attend(): return jnp.concatenate(outputs, axis=0)[None]]
    all_gather x1, starting transfers between devices: 10.8 us -> 0.21 us  [shards(): terms = add_down(hidden, lax.all_gather(w_down, 'seq', axis=0, tiled=True))]
    unnamed x4 -> x3, other arithmetic: 56 us -> 45.6 us
    unnamed x47 -> x59, local copies, waits for them, and re-layouts: 21 us -> 26.9 us
  transfers between devices with their start and end apart: 8 -> 8, of which waited for: 5 -> 5; matrix products, arithmetic and copies ran while one was open for 33% -> 28% of each run, Pallas kernels for 0% -> 0%
where the time goes in v1:
time: 405 us; the launch traced here: 397 us
  waiting for transfers between devices  190 us (47%)
  other arithmetic  65 us (16%)
  local copies, waits for them, and re-layouts  54.6 us (13%)
  matrix products  45.6 us (11%)
  starting transfers between devices  28.2 us (7%)
  between operations  13.9 us (3%)
    all_gather x1, waiting for transfers between devices, shards(): lax.all_gather(w_in, 'seq', axis=1, tiled=True)  72.1 us
    reduce_scatter x1, waiting for transfers between devices, shards(): lax.psum_scatter(terms.astype(jnp.bfloat16), 'grp', scatter_dimension=0,...  61.5 us
    unnamed x3, other arithmetic  45.6 us
    all_gather x1, waiting for transfers between devices, shards(): gathered = lax.all_gather(dispatched, 'grp', axis=0, tiled=True)  38.5 us
    unnamed x59, local copies, waits for them, and re-layouts  26.9 us
    dot_general x1, matrix products, project_in(): jnp.einsum('rd,khd->krh', gathered, piece, preferred_element_type=jnp.flo...  18.6 us
    all_to_all x1, waiting for transfers between devices, swap_blocks(): blocks = lax.all_to_all(blocks, mesh_axis, split_axis=0, concat_axis=0)  13.6 us
    dot_general x4, matrix products, attend(): jnp.einsum('kgqt,tkd->qkgd', weights.astype(jnp.bfloat16), value_split, p...  11.1 us
  transfers between devices with their start and end apart: 8, of which 5 were waited for; matrix products, arithmetic and copies ran while one was open for 28% of the time, Pallas kernels for 0%

profile of v1, /device:TPU:2, one launch (start us, length us, event | category | flops | bytes accessed | tf_op | source)
XLA Modules:
  0.0 397.3 jit_solution(17470519598905034944)
XLA Ops:
  6.5 1.2 copy.76
  7.9 8.1 %copy.105 = bf16[1,128,2048]{1,0,2:T(2,128)(2,1)S(1)} copy(bf16[1,128,2048]{1,2,0:T(8,128)(2,1)S(1)} %bitcast.359) | data formatting | bytes 1048576 | tf_op jit(solution)/shard_map/broadcast_in_dim | solution.py:84
  16.6 11.6 %reduce.17 = bf16[2048,128]{1,0:T(8,128)(2,1)S(1)} reduce(bf16[2048,1,128]{2,1,0:T(2,128)(2,1)S(1)} %bitcast.357, bf16[]{:T(256)} %broadcast.226), dimensions={1}, to_apply=%bitcast.350.reduce_sub_computation | reduce | bytes 1048578
  28.2 0.9 reshape.323
  29.1 7.5 %all-to-all-start = ((bf16[16,2,8192]{2,1,0:T(2,128)(2,1)}), bf16[16,2,8192]{2,1,0:T(2,128)(2,1)S(1)}, u32[]{:S(2)}, u32[]{:S(2)}) async-start(bf16[16,2,8192]{2,1,0:T(2,128)(2,1)} %reshape.323), calls=%async_computation | async-start | bytes 1048576 | tf_op jit(solution)/shard_map/all_to_all | solution.py:92
  37.3 1.1 copy.77
  38.5 8.1 %copy.104 = bf16[1,128,2048]{1,0,2:T(2,128)(2,1)S(1)} copy(bf16[1,128,2048]{1,2,0:T(8,128)(2,1)S(1)} %bitcast.360) | data formatting | bytes 1048576 | tf_op jit(solution)/shard_map/broadcast_in_dim | solution.py:87
  46.7 11.6 %reduce.16 = bf16[2048,128]{1,0:T(8,128)(2,1)S(1)} reduce(bf16[2048,1,128]{2,1,0:T(2,128)(2,1)S(1)} %bitcast.358, bf16[]{:T(256)} %broadcast.226), dimensions={1}, to_apply=%bitcast.349.reduce_sub_computation | reduce | bytes 1048578
  58.3 0.9 reshape.321
  59.2 7.2 %all-to-all-start.2 = ((bf16[16,2,8192]{2,1,0:T(2,128)(2,1)}), bf16[16,2,8192]{2,1,0:T(2,128)(2,1)}, u32[]{:S(2)}, u32[]{:S(2)}) async-start(bf16[16,2,8192]{2,1,0:T(2,128)(2,1)} %reshape.321), calls=%async_computation.2 | async-start | bytes 1048576 | tf_op jit(solution)/shard_map/all_to_all | solution.py:93
  66.5 2.8 copy.53
  69.3 22.4 %reduce.18 = bf16[4096,128]{1,0:T(8,128)(2,1)S(1)} reduce(bf16[4096,1,128]{2,1,0:T(2,128)(2,1)S(1)} %bitcast.352, bf16[]{:T(256)} %broadcast.226), dimensions={1}, to_apply=%bitcast.335.reduce_sub_computation | reduce | bytes 2097154
  91.7 1.1 reshape.325
  93.0 7.7 %all-to-all-start.1 = ((bf16[16,2,16384]{2,1,0:T(2,128)(2,1)}), bf16[16,2,16384]{2,1,0:T(2,128)(2,1)S(1)}, u32[]{:S(2)}, u32[]{:S(2)}) async-start(bf16[16,2,16384]{2,1,0:T(2,128)(2,1)} %reshape.325), calls=%async_computation.1 | async-start | bytes 2097152 | tf_op jit(solution)/shard_map/all_to_all | solution.py:91
  100.8 3.8 broadcast_compare_fusion.3
  104.6 2.2 reshape.324
  106.9 1.0 copy.52
  108.0 2.2 reshape.322
  110.6 1.0 reshape.316
  111.6 3.1 all-to-all-done.1
  114.7 1.0 reshape.326
  116.5 3.3 fusion.10
  119.8 2.0 fusion
  121.8 2.6 fusion.59
  124.5 2.2 fusion.11
  126.7 2.2 fusion.2
  128.9 3.3 fusion.65
  132.4 2.2 fusion.12
  134.7 2.0 fusion.4
  136.7 2.6 fusion.71
  139.5 2.2 fusion.13
  141.8 2.0 fusion.6
  143.8 2.6 fusion.77
  156.9 5.5 %all-to-all-start.3 = ((bf16[16,1,128,256]{2,3,1,0:T(8,128)(2,1)}), bf16[16,1,128,256]{2,3,1,0:T(8,128)(2,1)S(1)}, u32[]{:S(2)}, u32[]{:S(2)}) async-start(bf16[16,1,128,256]{2,3,1,0:T(8,128)(2,1)} %fusion.91), calls=%async_computation.3 | async-start | bytes 2097152 | tf_op jit(solution)/shard_map/all_to_all | solution.py:19
  162.9 13.6 %all-to-all-done.3 = bf16[16,1,128,256]{2,3,1,0:T(8,128)(2,1)S(1)} async-done(((bf16[16,1,128,256]{2,3,1,0:T(8,128)(2,1)}), bf16[16,1,128,256]{2,3,1,0:T(8,128)(2,1)S(1)}, u32[]{:S(2)}, u32[]{:S(2)}) %all-to-all-start.3) | async-done | bytes 1048608 | tf_op jit(solution)/shard_map/all_to_all | solution.py:19
  177.1 0.7 fusion.32
  177.8 1.2 convolution_convert_fusion.1
  179.8 5.0 %reshape.314 = bf16[448,4096]{1,0:T(8,128)(2,1)} reshape(bf16[16,28,4096]{2,1,0:T(8,128)(2,1)} %all-gather.9.cloned.1.call-done) | data formatting | bytes 7340032
  184.8 38.5 %all-gather.5.cloned.1.call-done = bf16[640,4096]{1,0:T(8,128)(2,1)} async-done(((bf16[40,4096]{1,0:T(8,128)(2,1)}), bf16[640,4096]{1,0:T(8,128)(2,1)}) %all-gather.5.cloned.1.call-update) | async-done | bytes 5242896 | tf_op jit(solution)/shard_map/all_gather | solution.py:109
  223.3 72.1 %all-gather.7.cloned.1.call-done = bf16[2,448,4096]{2,0,1:T(2,128)(2,1)} async-done(((bf16[2,28,4096]{2,0,1:T(2,128)(2,1)}), bf16[2,448,4096]{2,0,1:T(2,128)(2,1)}) %all-gather.7.cloned.1.call-update) | async-done | bytes 7340048 | tf_op jit(solution)/shard_map/all_gather | solution.py:110
  295.4 18.6 %fusion.37 = f32[2,640,448]{1,2,0:T(8,128)S(1)} fusion(bf16[2,448,4096]{2,0,1:T(2,128)(2,1)} %all-gather.7.cloned.1.call-done, bf16[640,4096]{1,0:T(8,128)(2,1)} %all-gather.5.cloned.1.call-done), kind=kOutput, calls=%fused_computation.51 | convolution fusion | flops 4697620480 | bytes 14876672 | tf_op jit(solution)/shard_map/rd,khd->krh/dot_general | solution.py:24
  314.0 4.8 %convolution_convert_fusion = bf16[640,4096]{1,0:T(8,128)(2,1)} fusion(bf16[448,4096]{1,0:T(8,128)(2,1)S(1)} %copy-done.4, f32[2,640,448]{1,2,0:T(8,128)S(1)} %fusion.37), kind=kOutput, calls=%fused_computation.23 | convolution fusion | flops 2353152000 | bytes 11206656 | tf_op jit(solution)/shard_map/dot_general | solution.py:32
  318.9 1.6 convert_element_type.130
  320.4 1.9 copy.78
  322.4 61.5 %reduce-scatter.2.cloned.1.call-done = bf16[40,4096]{1,0:T(8,128)(2,1)} async-done(((bf16[640,4096]{1,0:T(8,128)(2,1)}), bf16[40,4096]{1,0:T(8,128)(2,1)}) %reduce-scatter.2.cloned.1.call-update) | async-done | bytes 327696 | tf_op jit(solution)/shard_map/reduce_scatter | solution.py:113
  383.8 1.0 convert_element_type.125
  384.9 2.6 gather_fusion
  387.4 3.1 fusion.36
  (90 shorter events, 15.8 us)
Async XLA Ops:
  6.5 59.9 %copy-start.13 = (s32[1,16]{1,0:T(1,128)S(1)}, s32[1,16]{1,0:T(1,128)}, u32[]{:S(2)}) copy-start(s32[1,16]{1,0:T(1,128)} %param.12) | copy-start | bytes 196
  6.5 60.0 %copy-start.6 = (bf16[1,128,4096]{2,1,0:T(8,128)(2,1)S(1)}, bf16[1,128,4096]{2,1,0:T(8,128)(2,1)}, u32[]{:S(2)}) copy-start(bf16[1,128,4096]{2,1,0:T(8,128)(2,1)} %param.9) | copy-start | bytes 3145732
  29.1 30.1 %all-to-all-start = ((bf16[16,2,8192]{2,1,0:T(2,128)(2,1)}), bf16[16,2,8192]{2,1,0:T(2,128)(2,1)S(1)}, u32[]{:S(2)}, u32[]{:S(2)}) async-start(bf16[16,2,8192]{2,1,0:T(2,128)(2,1)} %reshape.323), calls=%async_computation | async-start | bytes 1048576 | tf_op jit(solution)/shard_map/all_to_all | solution.py:92
  36.6 143.2 %all-gather.9.cloned.1.call-start = ((), (), s32[]{:S(2)}) async-start(), calls=%async_computation.8 | async-start | bytes 4456448 | tf_op jit(solution)/shard_map/all_gather | solution.py:112
  59.2 7.2 %copy-start.5 = (bf16[16,2,8192]{2,1,0:T(2,128)(2,1)}, bf16[16,2,8192]{2,1,0:T(2,128)(2,1)S(1)}, u32[]{:S(2)}) copy-start(bf16[16,2,8192]{2,1,0:T(2,128)(2,1)S(1)} %all-to-all-done) | copy-start | bytes 1572868
  59.2 33.8 %all-to-all-start.2 = ((bf16[16,2,8192]{2,1,0:T(2,128)(2,1)}), bf16[16,2,8192]{2,1,0:T(2,128)(2,1)}, u32[]{:S(2)}, u32[]{:S(2)}) async-start(bf16[16,2,8192]{2,1,0:T(2,128)(2,1)} %reshape.321), calls=%async_computation.2 | async-start | bytes 1048576 | tf_op jit(solution)/shard_map/all_to_all | solution.py:93
  93.0 21.7 %all-to-all-start.1 = ((bf16[16,2,16384]{2,1,0:T(2,128)(2,1)}), bf16[16,2,16384]{2,1,0:T(2,128)(2,1)S(1)}, u32[]{:S(2)}, u32[]{:S(2)}) async-start(bf16[16,2,16384]{2,1,0:T(2,128)(2,1)} %reshape.325), calls=%async_computation.1 | async-start | bytes 2097152 | tf_op jit(solution)/shard_map/all_to_all | solution.py:91
  115.9 3.8 copy-start.3
  116.5 5.3 %copy-start.8 = (bf16[2048,128,1]{0,1,2:T(8,128)(2,1)S(1)}, bf16[2048,128,1]{0,1,2:T(8,128)(2,1)}, u32[]{:S(2)}) copy-start(bf16[2048,128,1]{0,1,2:T(8,128)(2,1)} %reshape.316) | copy-start | bytes 1572868
  121.8 2.6 copy-start.2
  121.8 2.6 copy-start.7
  128.9 3.5 copy-start.1
  132.4 4.2 %copy-start.9 = (bf16[2048,128,1]{0,1,2:T(8,128)(2,1)S(1)}, bf16[2048,128,1]{0,1,2:T(8,128)(2,1)}, u32[]{:S(2)}) copy-start(bf16[2048,128,1]{0,1,2:T(8,128)(2,1)} %reshape.316) | copy-start | bytes 1572868
  136.7 2.9 copy-start
  139.5 4.3 %copy-start.10 = (bf16[2048,128,1]{0,1,2:T(8,128)(2,1)S(1)}, bf16[2048,128,1]{0,1,2:T(8,128)(2,1)}, u32[]{:S(2)}) copy-start(bf16[2048,128,1]{0,1,2:T(8,128)(2,1)} %reshape.316) | copy-start | bytes 1572868
  143.8 2.7 copy-start.11
  143.8 18.7 %copy-start.14 = (s32[1,128,2]{1,2,0:T(2,128)S(1)}, s32[1,128,2]{1,2,0:T(2,128)}, u32[]{:S(2)}) copy-start(s32[1,128,2]{1,2,0:T(2,128)} %param.13) | copy-start | bytes 3076
  143.8 33.3 %copy-start.12 = (f32[4096]{0:T(1024)S(1)}, f32[4096]{0:T(1024)}, u32[]{:S(2)}) copy-start(f32[4096]{0:T(1024)} %param.15) | copy-start | bytes 49156
  156.9 19.6 %all-to-all-start.3 = ((bf16[16,1,128,256]{2,3,1,0:T(8,128)(2,1)}), bf16[16,1,128,256]{2,3,1,0:T(8,128)(2,1)S(1)}, u32[]{:S(2)}, u32[]{:S(2)}) async-start(bf16[16,1,128,256]{2,3,1,0:T(8,128)(2,1)} %fusion.91), calls=%async_computation.3 | async-start | bytes 2097152 | tf_op jit(solution)/shard_map/all_to_all | solution.py:19
  162.4 60.9 %all-gather.5.cloned.1.call-start = ((), (), s32[]{:S(2)}) async-start(), calls=%async_computation.5 | async-start | bytes 5570560 | tf_op jit(solution)/shard_map/all_gather | solution.py:109
  179.0 116.4 %all-gather.7.cloned.1.call-start = ((), (), s32[]{:S(2)}) async-start(), calls=%async_computation.6 | async-start | bytes 7798784 | tf_op jit(solution)/shard_map/all_gather | solution.py:110
  179.7 204.1 %reduce-scatter.2.cloned.1.call-start = ((), (), s32[]{:S(2)}) async-start(), calls=%async_computation.7 | async-start | bytes 5570560 | tf_op jit(solution)/shard_map/reduce_scatter | solution.py:113
  295.4 18.6 %copy-start.4 = (bf16[448,4096]{1,0:T(8,128)(2,1)S(1)}, bf16[448,4096]{1,0:T(8,128)(2,1)}, u32[]{:S(2)}) copy-start(bf16[448,4096]{1,0:T(8,128)(2,1)} %reshape.314) | copy-start | bytes 11010052
  314.0 4.8 %copy-start.15 = (f32[1,128,2]{1,2,0:T(2,128)S(1)}, f32[1,128,2]{1,2,0:T(2,128)}, u32[]{:S(2)}) copy-start(f32[1,128,2]{1,2,0:T(2,128)} %param.14) | copy-start | bytes 3076
Sparse Core Ops, SparseCore 0:
  39.8 59.1 all-gather.8
  179.1 44.1 all-gather.4
  225.8 69.6 all-gather.6
  318.9 64.8 reduce-scatter.1
